TPU v7x, 512 devices: a whole 4x4x16 slice. The times are simulated.
512 devices in a mesh: clip: 4 (over y), st: 32 (over x_hi, z), fsdp: 4 (over x_lo, core).
Axes of the slice: x: 4 (x_hi: 2, x_lo: 2; x = x_hi * 2 + x_lo), y: 4, z: 16, core: 2. Of those that a mesh axis runs over, the one named last changes fastest.
Arguments:
- clip_tokens: bfloat16 [1024, 128, 1024], P(('clip', 'st'), 'fsdp'), parts along dimension 0, may hold values from -6 to 6
- w_spatial: bfloat16 [9, 1024, 512], P(None, ('st', 'fsdp')), may hold values from -0.0625 to 0.0625
- w_temporal: bfloat16 [3, 512, 1024], P(None, None, ('st', 'fsdp')), may hold values from -0.15625 to 0.15625
- frame_time: int32 [64], P('clip'), parts along dimension 0, may hold values from 0 to 15, each once
- dilation: int32 [32], P('clip'), parts along dimension 0, may hold values from 1 to 3
Outputs:
- block_out: bfloat16 [1024, 128, 1024], P(('clip', 'st'), 'fsdp'), parts along dimension 0
There are 4 independent parts, one for each index of `clip`. A program takes and returns all parts, laid end to end along the dimension named above; an argument that names none is the same for every part. Nothing has to cross between parts.
Inputs may be any that keep to these rules, and one draw needn't show every extreme that they name: frame_time is a permutation of 0 to 15.
All inputs are finite; a program needn't handle non-finite values.
Results may differ from a plain program's by a relative error of at most 0.0049.
Values may be sent and summed in bfloat16 or wider, within the bound.
No kernel may reach another device: no remote copies, remote signals or barrier semaphores. Data moves between devices by JAX's collectives and lax.ppermute only.
A program may use at most 64 MiB of HBM per device.

v0:
```python
import jax
import jax.numpy as jnp
from jax import lax
from jax.sharding import PartitionSpec as P

DGROUPS = 8
FRAMES = 16
ROWS = 16
ST = ("xhi", "zhi", "zlo")
FS = ("xlo", "core")
FRAME_AXES = ("xhi", "zhi")
ALL = ("xhi", "zhi", "zlo", "xlo", "core")


def padded_2(cells, sides, width):
    for axis, dim in sides:
        count = lax.axis_size(axis)
        ends = count - 1
        head = lax.slice_in_dim(cells, 0, width, axis=dim)
        tail = lax.slice_in_dim(cells, cells.shape[dim] - width, cells.shape[dim], axis=dim)
        cells = jnp.concatenate(
            [
                lax.ppermute(tail, axis, [(i, (i + 1) % count) for i in range(ends)]),
                cells,
                lax.ppermute(head, axis, [((i + 1) % count, i) for i in range(ends)]),
            ],
            axis=dim,
        )
    return cells


def partner(value, axis, distance):
    mask = 2**distance
    pairs = [(source, source ^ mask) for source in range(lax.axis_size(axis))]
    return lax.ppermute(value, axis, pairs)


def weight_rows(w_spatial, w_temporal):
    middle = w_spatial.shape[2]
    return jnp.concatenate(
        [w_spatial.reshape(-1, middle), w_temporal.transpose(2, 0, 1).reshape(-1, middle)], axis=0
    )


def channel_dims():
    return (
        lax.axis_size("xhi"),
        lax.axis_size("zhi") * lax.axis_size("zlo"),
        lax.axis_size("xlo"),
        lax.axis_size("core"),
    )


def to_gathered_order(cells, block):
    lead = cells.shape[:-1]
    n = len(lead)
    split = cells.reshape(lead + channel_dims() + (block,))
    order = tuple(range(n)) + (n + 3, n, n + 2, n + 1, n + 4)
    return split.transpose(order).reshape(lead + (-1, block))


def from_gathered_order(cells, block):
    lead = cells.shape[:-1]
    n = len(lead)
    xhi, z, xlo, core = channel_dims()
    split = cells.reshape(lead + (core, xhi, xlo, z, block))
    order = tuple(range(n)) + (n + 1, n + 3, n + 2, n, n + 4)
    return split.transpose(order).reshape(lead + (-1,))


def shards(clip_tokens, w_spatial, w_temporal, frame_time, dilation):
    rows_dev, cols_dev, channels = clip_tokens.shape
    middle = w_spatial.shape[2]
    block_in = w_spatial.shape[1]
    block_out = w_temporal.shape[2]
    spatial_rows = w_spatial.shape[0] * block_in
    along_z = lax.all_gather(weight_rows(w_spatial, w_temporal), ("zhi", "zlo"), axis=0)
    values = clip_tokens.astype(jnp.float32)
    average = jnp.mean(values, axis=-1, keepdims=True)
    kernel_extent = jnp.mean(jnp.square(values - average), axis=-1, keepdims=True)
    normed = ((values - average) * lax.rsqrt(kernel_extent + 1e-06)).astype(jnp.bfloat16)
    normed = to_gathered_order(normed, block_in).reshape(rows_dev, cols_dev, channels)
    widened = padded_2(normed, ((FS, 1),), 1)
    blank_row = jnp.zeros((1,) + widened.shape[1:], jnp.bfloat16)
    lower_half = lax.axis_index(ST) % 2 == 1
    outgoing = jnp.where(lower_half, widened[:1], widened[-1:])
    incoming = partner(outgoing, ST, 0)
    top_rim = jnp.where(lower_half, incoming, blank_row)
    bottom_rim = jnp.where(lower_half, blank_row, incoming)
    padded = jnp.concatenate([top_rim, widened, bottom_rim], axis=0)
    first_row = lax.axis_index(ST) * rows_dev
    in_frame = (first_row + jnp.arange(rows_dev, dtype=jnp.int32)) % ROWS
    masks = []
    for shift_amount in (-1, 0, 1):
        masks.append(
            ((in_frame + shift_amount >= 0) & (in_frame + shift_amount < ROWS)).astype(jnp.bfloat16)
        )
    tokens = rows_dev * cols_dev
    other_core = [(0, 1), (1, 0)]
    partner_padded = lax.ppermute(padded, "core", other_core)
    half_blocks = channels // block_in // lax.axis_size("core")
    start = lax.axis_index("core") * half_blocks
    width = half_blocks * block_in
    own_part = lax.dynamic_slice_in_dim(padded, start * block_in, width, axis=2)
    partner_part = lax.dynamic_slice_in_dim(partner_padded, start * block_in, width, axis=2)
    patches = []
    for row_tap in range(3):
        inside = masks[row_tap][:, None, None]
        mine = own_part[row_tap : row_tap + rows_dev] * inside
        theirs = partner_part[row_tap : row_tap + rows_dev] * inside
        for column_kernel_tap in range(3):
            both = jnp.concatenate(
                [
                    src_tile[:, column_kernel_tap : column_kernel_tap + cols_dev, :]
                    for src_tile in (mine, theirs)
                ]
            )
            patches.append(both.reshape(2 * tokens, width))
    early = 3
    along_z, *head = lax.optimization_barrier((along_z, *patches[:early]))
    patches[:early] = head
    own_half = lax.all_gather(along_z[:, :spatial_rows], ("xhi", "xlo"), axis=0)
    own_half = own_half.reshape((-1, spatial_rows) + along_z.shape[2:])
    temporal_rows = along_z[:, spatial_rows:]
    partial = jnp.zeros((2 * tokens, middle), jnp.float32)
    for tap, patch in enumerate(patches):
        partial = partial + jnp.dot(
            patch,
            own_half[:, tap * block_in : (tap + 1) * block_in, :].reshape(width, middle),
            preferred_element_type=jnp.float32,
        )
    partial, temporal_rows = lax.optimization_barrier((partial, temporal_rows))
    temporal_rows = lax.all_gather(temporal_rows, ("xhi", "xlo"), axis=0)
    running = partial[:tokens] + lax.ppermute(partial[tokens:], "core", other_core)
    hidden = jax.nn.gelu(running).astype(jnp.bfloat16)
    group_size = lax.axis_size(FRAME_AXES)
    per_pixel = tokens // group_size
    arrived = lax.all_to_all(
        hidden.reshape(group_size, per_pixel, middle), FRAME_AXES, 0, 0, tiled=True
    )
    group_width = middle // DGROUPS
    frame_sequence = arrived.reshape(FRAMES, per_pixel, DGROUPS, group_width)
    offsets = (jnp.arange(3, dtype=jnp.int32) - 1)[None, :] * dilation[:, None]
    selector_matrix = (
        frame_time[None, None, None, :]
        == frame_time[None, None, :, None] + offsets[:, :, None, None]
    ).astype(jnp.bfloat16)
    stacked_panels = jnp.einsum(
        "gkfe,epgc->fpkgc", selector_matrix, frame_sequence, preferred_element_type=jnp.float32
    )
    stacked_panels = stacked_panels.astype(jnp.bfloat16).reshape(FRAMES * per_pixel, 3, middle)
    xhi, z, xlo, core = channel_dims()
    arrived, temporal_rows = lax.optimization_barrier((arrived, temporal_rows))
    pair = jnp.stack([temporal_rows, lax.ppermute(temporal_rows, "core", other_core)])
    temporal_w = jnp.where(lax.axis_index("core") == 0, pair, pair[::-1])
    temporal_w = temporal_w.reshape(core, xhi, xlo, z, block_out, 3, middle)
    temporal_w = temporal_w.transpose(1, 3, 2, 0, 4, 5, 6).reshape(channels, 3, middle)
    result = lax.dot_general(
        stacked_panels, temporal_w, (((1, 2), (1, 2)), ((), ())), preferred_element_type=jnp.float32
    )
    mixed_out = result.astype(jnp.bfloat16)
    returned = lax.all_to_all(
        mixed_out.reshape(group_size, per_pixel, channels), FRAME_AXES, 0, 0, tiled=True
    )
    update = returned.reshape(rows_dev, cols_dev, channels)
    return (values + update.astype(jnp.float32)).astype(jnp.bfloat16)


def solution(mesh):
    clips = mesh.shape["clip"]
    fine = jax.sharding.Mesh(
        mesh.devices.reshape(clips, 2, -1, 2, 2, 2), ("clip",) + ALL
    )
    return jax.shard_map(
        shards,
        mesh=fine,
        in_specs=(
            P(("clip",) + ST, FS, None),
            P(None, ALL, None),
            P(None, None, ALL),
            P("clip"),
            P("clip"),
        ),
        out_specs=P(("clip",) + ST, FS, None),
        check_vma=False,
    )
```

profile of v0, /device:TPU:1, one launch (start us, length us, event | category | flops | bytes accessed | tf_op | source)
XLA Modules:
  0.0 251.6 jit_solution(1425399597807551591)
XLA Ops:
  7.3 1.5 pad_maximum_fusion.12
  12.8 1.8 copy.62
  14.5 2.2 copy.63
  16.7 2.7 %fusion.22 = (bf16[8,1,1024]{1,2,0:T(8,128)(2,1)}, bf16[8,1,1024]{1,2,0:T(8,128)(2,1)}) fusion(bf16[8,32,1024]{1,2,0:T(8,128)(2,1)S(1)} %bitcast.83), kind=kLoop, calls=%fused_computation.79 | loop fusion | bytes 65536 | tf_op jit(solution)/shard_map/slice | solution.py:20
  19.4 2.0 copy.64
  21.4 4.5 %collective-permute-start = (bf16[8,1,1024]{2,0,1:T(8,128)(2,1)S(1)}, bf16[8,1,1024]{2,0,1:T(8,128)(2,1)S(1)}, u32[]{:S(2)}, u32[]{:S(2)}) collective-permute-start(bf16[8,1,1024]{2,0,1:T(8,128)(2,1)S(1)} %copy.64), channel_id=1, source_target_pairs={{0,1},{1,2},{2,3},{4,5},{5,6},{6,7},{8,9},{9,10},{10,11},{12,13},{... | collective-permute-start | bytes 49160 | tf_op jit(solution)/shard_map/ppermute | solution.py:23
  25.9 2.0 copy.65
  27.9 5.6 %collective-permute-start.1 = (bf16[8,1,1024]{2,0,1:T(8,128)(2,1)S(1)}, bf16[8,1,1024]{2,0,1:T(8,128)(2,1)S(1)}, u32[]{:S(2)}, u32[]{:S(2)}) collective-permute-start(bf16[8,1,1024]{2,0,1:T(8,128)(2,1)S(1)} %copy.65), channel_id=1, source_target_pairs={{1,0},{2,1},{3,2},{5,4},{6,5},{7,6},{9,8},{10,9},{11,10},{13,12},{... | collective-permute-start | bytes 49160 | tf_op jit(solution)/shard_map/ppermute | solution.py:25
  33.5 1.8 copy.66
  35.3 1.9 copy.67
  37.2 4.1 %pad_maximum_fusion.1 = bf16[8,34,1024]{1,2,0:T(8,128)(2,1)S(1)} fusion(bf16[8,1,1024]{1,2,0:T(8,128)(2,1)} %copy.67, bf16[8,32,1024]{1,2,0:T(8,128)(2,1)S(1)} %bitcast.84, bf16[8,1,1024]{1,2,0:T(8,128)(2,1)} %copy.66), kind=kLoop, calls=%fused_computation.2 | loop fusion | flops 1671168 | bytes 1114112 | tf_op jit(solution)/shard_map/concatenate | solution.py:21
  41.4 1.3 copy-done
  42.7 1.9 collective-permute-start.2
  44.7 2.0 copy.69
  46.7 8.1 %collective-permute-done.2 = bf16[1,34,1024]{1,2,0:T(8,128)(2,1)S(1)} collective-permute-done((bf16[1,34,1024]{1,2,0:T(8,128)(2,1)S(1)}, bf16[1,34,1024]{1,2,0:T(8,128)(2,1)S(1)}, u32[]{:S(2)}, u32[]{:S(2)}) %collective-permute-start.2) | collective-permute-done | bytes 69664 | tf_op jit(solution)/shard_map/ppermute | solution.py:35
  55.3 1.9 collective-permute-start.3
  57.3 2.3 collective-permute-done.3
  60.8 17.8 %all-gather.7.cloned.1.call-done = bf16[1536,512]{1,0:T(8,128)(2,1)} async-done(((bf16[96,512]{1,0:T(8,128)(2,1)}), bf16[1536,512]{1,0:T(8,128)(2,1)}) %all-gather.7.cloned.1.call-update) | async-done | bytes 1572880 | tf_op jit(solution)/shard_map/all_gather | solution.py:77
  78.6 2.4 slice.135
  85.9 1.8 slice.161
  87.7 59.4 %all-gather.9.cloned.1.call-done = bf16[64,72,512]{2,1,0:T(8,128)(2,1)} async-done(((bf16[16,72,512]{2,1,0:T(8,128)(2,1)}), bf16[64,72,512]{2,1,0:T(8,128)(2,1)}) %all-gather.9.cloned.1.call-update) | async-done | bytes 4718608 | tf_op jit(solution)/shard_map/all_gather | solution.py:122
  147.1 1.6 fusion.15
  148.7 1.5 convolution_add_fusion.7
  153.9 2.6 %collective-permute-start.4 = (f32[256,512]{1,0:T(8,128)S(1)}, f32[256,512]{1,0:T(8,128)S(1)}, u32[]{:S(2)}, u32[]{:S(2)}) collective-permute-start(f32[256,512]{1,0:T(8,128)S(1)} %slice.163), channel_id=1, source_target_pairs={{0,1},{1,0},{2,3},{3,2},{4,5},{5,4},{6,7},{7,6},{8,9},{9,8},{10,11... | collective-permute-start | bytes 1572872 | tf_op jit(solution)/shard_map/ppermute | solution.py:134
  156.5 1.5 collective-permute-done.4
  158.2 29.4 %all_to_all.10 = bf16[16,16,512]{2,1,0:T(8,128)(2,1)S(1)} all-to-all(bf16[16,16,512]{2,1,0:T(8,128)(2,1)S(1)} %bitcast.103), channel_id=1, replica_groups=mesh['clip'=4,'xhi'=2,'zhi'=8,'zlo'=2,'xlo'=2,'core'=2] {'xhi','zhi'}, dimensions={0} | all-to-all | bytes 524288 | tf_op jit(solution)/shard_map/all_to_all | solution.py:138
  187.6 3.9 %all-gather.11.cloned.1.call-done = bf16[64,24,512]{2,1,0:T(8,128)(2,1)} async-done(((bf16[16,24,512]{2,1,0:T(8,128)(2,1)}), bf16[64,24,512]{2,1,0:T(8,128)(2,1)}) %all-gather.11.cloned.1.call-update) | async-done | bytes 1572880 | tf_op jit(solution)/shard_map/all_gather | solution.py:133
  191.5 2.6 %collective-permute-start.5 = (bf16[4,16,24,512]{3,2,1,0:T(8,128)(2,1)}, bf16[4,16,24,512]{3,2,1,0:T(8,128)(2,1)}, u32[]{:S(2)}, u32[]{:S(2)}) collective-permute-start(bf16[4,16,24,512]{3,2,1,0:T(8,128)(2,1)} %bitcast.101), channel_id=1, source_target_pairs={{0,1},{1,0},{2,3},{3,2},{4,5},{5,4},{6,7},{7,6},{8,9},{9,8},{10,11... | collective-permute-start | bytes 4718600 | tf_op jit(solution)/shard_map/ppermute | solution.py:154
  196.5 1.7 reshape.196
  198.1 1.7 pad_maximum_fusion
  201.7 1.8 copy.74
  204.6 39.5 %all_to_all.11 = bf16[16,16,1024]{2,1,0:T(8,128)(2,1)S(1)} all-to-all(bf16[16,16,1024]{2,1,0:T(8,128)(2,1)S(1)} %bitcast.104), channel_id=1, replica_groups=mesh['clip'=4,'xhi'=2,'zhi'=8,'zlo'=2,'xlo'=2,'core'=2] {'xhi','zhi'}, dimensions={0} | all-to-all | bytes 1048576 | tf_op jit(solution)/shard_map/all_to_all | solution.py:162
  (81 shorter events, 21.3 us)
Async XLA Ops:
  6.5 72.1 %all-gather.7.cloned.1.call-start = ((), (), s32[]{:S(2)}) async-start(), calls=%async_computation.2 | async-start | bytes 1671168 | tf_op jit(solution)/shard_map/all_gather | solution.py:77
  8.9 138.2 %all-gather.9.cloned.1.call-start = ((), (), s32[]{:S(2)}) async-start(), calls=%async_computation.3 | async-start | bytes 5898240 | tf_op jit(solution)/shard_map/all_gather | solution.py:122
  21.4 12.1 %collective-permute-start = (bf16[8,1,1024]{2,0,1:T(8,128)(2,1)S(1)}, bf16[8,1,1024]{2,0,1:T(8,128)(2,1)S(1)}, u32[]{:S(2)}, u32[]{:S(2)}) collective-permute-start(bf16[8,1,1024]{2,0,1:T(8,128)(2,1)S(1)} %copy.64), channel_id=1, source_target_pairs={{0,1},{1,2},{2,3},{4,5},{5,6},{6,7},{8,9},{9,10},{10,11},{12,13},{... | collective-permute-start | bytes 49160 | tf_op jit(solution)/shard_map/ppermute | solution.py:23
  27.9 7.4 %collective-permute-start.1 = (bf16[8,1,1024]{2,0,1:T(8,128)(2,1)S(1)}, bf16[8,1,1024]{2,0,1:T(8,128)(2,1)S(1)}, u32[]{:S(2)}, u32[]{:S(2)}) collective-permute-start(bf16[8,1,1024]{2,0,1:T(8,128)(2,1)S(1)} %copy.65), channel_id=1, source_target_pairs={{1,0},{2,1},{3,2},{5,4},{6,5},{7,6},{9,8},{10,9},{11,10},{13,12},{... | collective-permute-start | bytes 49160 | tf_op jit(solution)/shard_map/ppermute | solution.py:25
  41.4 1.3 copy-start
  42.7 12.1 %collective-permute-start.2 = (bf16[1,34,1024]{1,2,0:T(8,128)(2,1)S(1)}, bf16[1,34,1024]{1,2,0:T(8,128)(2,1)S(1)}, u32[]{:S(2)}, u32[]{:S(2)}) collective-permute-start(bf16[1,34,1024]{1,2,0:T(8,128)(2,1)S(1)} %slice_select_fusion), channel_id=1, source_target_pairs={{0,4},{4,0},{8,12},{12,8},{16,20},{20,16},{24,28},{28,24},{32,36},... | collective-permute-start | bytes 208904 | tf_op jit(solution)/shard_map/ppermute | solution.py:35
  55.3 4.2 %collective-permute-start.3 = (bf16[10,34,1024]{2,1,0:T(8,128)(2,1)S(1)}, bf16[10,34,1024]{2,1,0:T(8,128)(2,1)S(1)}, u32[]{:S(2)}, u32[]{:S(2)}) collective-permute-start(bf16[10,34,1024]{2,1,0:T(8,128)(2,1)S(1)} %pad_maximum_fusion.2), channel_id=1, source_target_pairs={{0,1},{1,0},{2,3},{3,2},{4,5},{5,4},{6,7},{7,6},{8,9},{9,8},{10,11... | collective-permute-start | bytes 2088968 | tf_op jit(solution)/shard_map/ppermute | solution.py:100
  81.0 110.5 %all-gather.11.cloned.1.call-start = ((), (), s32[]{:S(2)}) async-start(), calls=%async_computation.4 | async-start | bytes 1966080 | tf_op jit(solution)/shard_map/all_gather | solution.py:133
  147.1 3.2 %copy-start.2 = (bf16[64,72,512]{2,1,0:T(8,128)(2,1)S(1)}, bf16[64,72,512]{2,1,0:T(8,128)(2,1)}, u32[]{:S(2)}) copy-start(bf16[64,72,512]{2,1,0:T(8,128)(2,1)} %all-gather.9.cloned.1.call-done) | copy-start | bytes 14155780
  148.7 2.0 copy-start.5
  150.3 1.0 copy-start.3
  151.3 1.0 copy-start.7
  151.7 1.1 copy-start.6
  152.3 1.1 copy-start.4
  153.4 40.7 %copy-start.11 = (s32[8]{0:T(128)S(1)}, s32[8]{0:T(128)}, u32[]{:S(2)}) copy-start(s32[8]{0:T(128)} %param.9) | copy-start | bytes 100
  153.4 40.8 %copy-start.10 = (s32[16]{0:T(128)S(1)}, s32[16]{0:T(128)}, u32[]{:S(2)}) copy-start(s32[16]{0:T(128)} %param.8) | copy-start | bytes 196
  153.9 4.1 %collective-permute-start.4 = (f32[256,512]{1,0:T(8,128)S(1)}, f32[256,512]{1,0:T(8,128)S(1)}, u32[]{:S(2)}, u32[]{:S(2)}) collective-permute-start(f32[256,512]{1,0:T(8,128)S(1)} %slice.163), channel_id=1, source_target_pairs={{0,1},{1,0},{2,3},{3,2},{4,5},{5,4},{6,7},{7,6},{8,9},{9,8},{10,11... | collective-permute-start | bytes 1572872 | tf_op jit(solution)/shard_map/ppermute | solution.py:134
  191.5 6.7 %collective-permute-start.5 = (bf16[4,16,24,512]{3,2,1,0:T(8,128)(2,1)}, bf16[4,16,24,512]{3,2,1,0:T(8,128)(2,1)}, u32[]{:S(2)}, u32[]{:S(2)}) collective-permute-start(bf16[4,16,24,512]{3,2,1,0:T(8,128)(2,1)} %bitcast.101), channel_id=1, source_target_pairs={{0,1},{1,0},{2,3},{3,2},{4,5},{5,4},{6,7},{7,6},{8,9},{9,8},{10,11... | collective-permute-start | bytes 4718600 | tf_op jit(solution)/shard_map/ppermute | solution.py:154
  195.4 2.7 %copy-start.8 = (bf16[64,24,512]{2,1,0:T(8,128)(2,1)S(1)}, bf16[64,24,512]{2,1,0:T(8,128)(2,1)}, u32[]{:S(2)}) copy-start(bf16[64,24,512]{2,1,0:T(8,128)(2,1)} %all-gather.11.cloned.1.call-done) | copy-start | bytes 4718596
  201.7 1.9 copy-start.9
  203.6 40.5 %copy-start.1 = (bf16[8,32,1024]{2,1,0:T(8,128)(2,1)S(1)}, bf16[8,32,1024]{2,1,0:T(8,128)(2,1)}, u32[]{:S(2)}) copy-start(bf16[8,32,1024]{2,1,0:T(8,128)(2,1)} %param.5) | copy-start | bytes 1572868
Sparse Core Ops, SparseCore 0:
  9.4 69.1 all-gather.6
  81.1 65.9 all-gather.8
  154.0 37.4 all-gather.10
where the time goes:
time: 255 us; the launch traced here: 252 us
  waiting for transfers between devices  93 us (36%)
  blocking collectives  68.9 us (27%)
  local copies, waits for them, and re-layouts  30.2 us (12%)
  starting transfers between devices  19.2 us (8%)
  other arithmetic  18.7 us (7%)
  between operations  13.6 us (5%)
  matrix products  8.06 us (3%)
    all_gather x1, waiting for transfers between devices, shards(): own_half = lax.all_gather(along_z[:, :spatial_rows], ('xhi', 'xlo'), axis=0)  59.4 us
    all_to_all x1, blocking collectives, shards(): lax.all_to_all(mixed_out.reshape(group_size, per_pixel, channels), FRAME_...  39.5 us
    all_to_all x1, blocking collectives, shards(): lax.all_to_all(hidden.reshape(group_size, per_pixel, middle), FRAME_AXES,...  29.4 us
    all_gather x1, waiting for transfers between devices, shards(): lax.all_gather(weight_rows(w_spatial, w_temporal), ('zhi', 'zlo'), axis=0)  17.8 us
    ppermute x1, waiting for transfers between devices, partner(): return lax.ppermute(value, axis, pairs)  8.1 us
    dot_general x9, matrix products, shards(): jnp.dot(patch, own_half[:, tap * block_in:(tap + 1) * block_in, :].reshap...  6.19 us
    ppermute x1, starting transfers between devices, padded_2(): lax.ppermute(head, axis, [((i + 1) % count, i) for i in range(ends)])  5.57 us
  transfers between devices with their start and end apart: 9, of which 6 were waited for; matrix products, arithmetic and copies ran while one was open for 15% of the time, Pallas kernels for 0%

commit v1 on v0

--- a/solution.py
+++ b/solution.py
@@ -150,7 +150,7 @@
     )
     stacked_panels = stacked_panels.astype(jnp.bfloat16).reshape(FRAMES * per_pixel, 3, middle)
     xhi, z, xlo, core = channel_dims()
-    arrived, temporal_rows = lax.optimization_barrier((arrived, temporal_rows))
+    stacked_panels, temporal_rows = lax.optimization_barrier((stacked_panels, temporal_rows))
     pair = jnp.stack([temporal_rows, lax.ppermute(temporal_rows, "core", other_core)])
     temporal_w = jnp.where(lax.axis_index("core") == 0, pair, pair[::-1])
     temporal_w = temporal_w.reshape(core, xhi, xlo, z, block_out, 3, middle)

time: 255 us -> 255 us (level)
  blocking collectives: 68.9 us -> 35.7 us
  starting transfers between devices: 19.2 us -> 36.5 us
  waiting for transfers between devices: 93 us -> 108 us
    all_to_all x1 -> x0, blocking collectives: 29.4 us -> none  [shards(): lax.all_to_all(hidden.reshape(group_size, per_pixel, middle), FRAME_AXES,...]
    all_to_all x0 -> x1, waiting for transfers between devices: none -> 15.8 us  [shards(): lax.all_to_all(hidden.reshape(group_size, per_pixel, middle), FRAME_AXES,...]
    all_to_all x0 -> x1, starting transfers between devices: none -> 13.6 us  [shards(): lax.all_to_all(hidden.reshape(group_size, per_pixel, middle), FRAME_AXES,...]
    all_gather x1, waiting for transfers between devices: 3.89 us -> 0.02 us  [shards(): temporal_rows = lax.all_gather(temporal_rows, ('xhi', 'xlo'), axis=0)]
    all_to_all x1, blocking collectives: 39.5 us -> 35.7 us  [shards(): lax.all_to_all(mixed_out.reshape(group_size, per_pixel, channels), FRAME_...]
    ppermute x1, starting transfers between devices: 2.6 us -> 6.28 us  [shards(): lax.ppermute(temporal_rows, 'core', other_core)]
    ppermute x1, waiting for transfers between devices: 0.01 us -> 3.22 us  [shards(): lax.ppermute(temporal_rows, 'core', other_core)]
  transfers between devices with their start and end apart: 9 -> 10, of which waited for: 6 -> 7; matrix products, arithmetic and copies ran while one was open for 15% -> 15% of each run, Pallas kernels for 0% -> 0%
where the time goes in v1:
time: 255 us; the launch traced here: 251 us
  waiting for transfers between devices  108 us (42%)
  starting transfers between devices  36.5 us (14%)
  blocking collectives  35.7 us (14%)
  local copies, waits for them, and re-layouts  29.5 us (12%)
  other arithmetic  19.4 us (8%)
  between operations  13.6 us (5%)
  matrix products  8.06 us (3%)
    all_gather x1, waiting for transfers between devices, shards(): own_half = lax.all_gather(along_z[:, :spatial_rows], ('xhi', 'xlo'), axis=0)  59.4 us
    all_to_all x1, blocking collectives, shards(): lax.all_to_all(mixed_out.reshape(group_size, per_pixel, channels), FRAME_...  35.7 us
    all_gather x1, waiting for transfers between devices, shards(): lax.all_gather(weight_rows(w_spatial, w_temporal), ('zhi', 'zlo'), axis=0)  17.8 us
    all_to_all x1, waiting for transfers between devices, shards(): lax.all_to_all(hidden.reshape(group_size, per_pixel, middle), FRAME_AXES,...  15.8 us
    all_to_all x1, starting transfers between devices, shards(): lax.all_to_all(hidden.reshape(group_size, per_pixel, middle), FRAME_AXES,...  13.6 us
    ppermute x1, waiting for transfers between devices, partner(): return lax.ppermute(value, axis, pairs)  8.1 us
    ppermute x1, starting transfers between devices, shards(): lax.ppermute(temporal_rows, 'core', other_core)  6.28 us
    dot_general x9, matrix products, shards(): jnp.dot(patch, own_half[:, tap * block_in:(tap + 1) * block_in, :].reshap...  6.19 us
  transfers between devices with their start and end apart: 10, of which 7 were waited for; matrix products, arithmetic and copies ran while one was open for 15% of the time, Pallas kernels for 0%

profile of v1, /device:TPU:1, one launch (start us, length us, event | category | flops | bytes accessed | tf_op | source)
XLA Modules:
  0.0 250.9 jit_solution(14678134626031339916)
XLA Ops:
  7.3 1.5 pad_maximum_fusion.12
  12.8 1.8 copy.62
  14.5 2.2 copy.63
  16.7 2.7 %fusion.22 = (bf16[8,1,1024]{1,2,0:T(8,128)(2,1)}, bf16[8,1,1024]{1,2,0:T(8,128)(2,1)}) fusion(bf16[8,32,1024]{1,2,0:T(8,128)(2,1)S(1)} %bitcast.83), kind=kLoop, calls=%fused_computation.79 | loop fusion | bytes 65536 | tf_op jit(solution)/shard_map/slice | solution.py:20
  19.4 2.0 copy.64
  21.4 4.5 %collective-permute-start = (bf16[8,1,1024]{2,0,1:T(8,128)(2,1)S(1)}, bf16[8,1,1024]{2,0,1:T(8,128)(2,1)S(1)}, u32[]{:S(2)}, u32[]{:S(2)}) collective-permute-start(bf16[8,1,1024]{2,0,1:T(8,128)(2,1)S(1)} %copy.64), channel_id=1, source_target_pairs={{0,1},{1,2},{2,3},{4,5},{5,6},{6,7},{8,9},{9,10},{10,11},{12,13},{... | collective-permute-start | bytes 49160 | tf_op jit(solution)/shard_map/ppermute | solution.py:23
  25.9 2.0 copy.65
  27.9 5.6 %collective-permute-start.1 = (bf16[8,1,1024]{2,0,1:T(8,128)(2,1)S(1)}, bf16[8,1,1024]{2,0,1:T(8,128)(2,1)S(1)}, u32[]{:S(2)}, u32[]{:S(2)}) collective-permute-start(bf16[8,1,1024]{2,0,1:T(8,128)(2,1)S(1)} %copy.65), channel_id=1, source_target_pairs={{1,0},{2,1},{3,2},{5,4},{6,5},{7,6},{9,8},{10,9},{11,10},{13,12},{... | collective-permute-start | bytes 49160 | tf_op jit(solution)/shard_map/ppermute | solution.py:25
  33.5 1.8 copy.66
  35.3 1.9 copy.67
  37.2 4.1 %pad_maximum_fusion.1 = bf16[8,34,1024]{1,2,0:T(8,128)(2,1)S(1)} fusion(bf16[8,1,1024]{1,2,0:T(8,128)(2,1)} %copy.67, bf16[8,32,1024]{1,2,0:T(8,128)(2,1)S(1)} %bitcast.84, bf16[8,1,1024]{1,2,0:T(8,128)(2,1)} %copy.66), kind=kLoop, calls=%fused_computation.2 | loop fusion | flops 1671168 | bytes 1114112 | tf_op jit(solution)/shard_map/concatenate | solution.py:21
  41.4 1.3 copy-done
  42.7 1.9 collective-permute-start.2
  44.7 2.0 copy.69
  46.7 8.1 %collective-permute-done.2 = bf16[1,34,1024]{1,2,0:T(8,128)(2,1)S(1)} collective-permute-done((bf16[1,34,1024]{1,2,0:T(8,128)(2,1)S(1)}, bf16[1,34,1024]{1,2,0:T(8,128)(2,1)S(1)}, u32[]{:S(2)}, u32[]{:S(2)}) %collective-permute-start.2) | collective-permute-done | bytes 69664 | tf_op jit(solution)/shard_map/ppermute | solution.py:35
  55.3 1.9 collective-permute-start.3
  57.3 2.3 collective-permute-done.3
  60.8 17.8 %all-gather.7.cloned.1.call-done = bf16[1536,512]{1,0:T(8,128)(2,1)} async-done(((bf16[96,512]{1,0:T(8,128)(2,1)}), bf16[1536,512]{1,0:T(8,128)(2,1)}) %all-gather.7.cloned.1.call-update) | async-done | bytes 1572880 | tf_op jit(solution)/shard_map/all_gather | solution.py:77
  78.6 2.4 slice.135
  85.9 1.8 slice.161
  87.7 59.4 %all-gather.9.cloned.1.call-done = bf16[64,72,512]{2,1,0:T(8,128)(2,1)} async-done(((bf16[16,72,512]{2,1,0:T(8,128)(2,1)}), bf16[64,72,512]{2,1,0:T(8,128)(2,1)}) %all-gather.9.cloned.1.call-update) | async-done | bytes 4718608 | tf_op jit(solution)/shard_map/all_gather | solution.py:122
  147.1 1.6 fusion.15
  148.7 1.5 convolution_add_fusion.7
  153.9 2.6 %collective-permute-start.4 = (f32[256,512]{1,0:T(8,128)S(1)}, f32[256,512]{1,0:T(8,128)S(1)}, u32[]{:S(2)}, u32[]{:S(2)}) collective-permute-start(f32[256,512]{1,0:T(8,128)S(1)} %slice.163), channel_id=1, source_target_pairs={{0,1},{1,0},{2,3},{3,2},{4,5},{5,4},{6,7},{7,6},{8,9},{9,8},{10,11... | collective-permute-start | bytes 1572872 | tf_op jit(solution)/shard_map/ppermute | solution.py:134
  156.5 1.5 collective-permute-done.4
  158.9 13.6 %all-to-all-start = ((bf16[16,16,512]{2,1,0:T(8,128)(2,1)}), bf16[16,16,512]{2,1,0:T(8,128)(2,1)S(1)}, u32[]{:S(2)}, u32[]{:S(2)}) async-start(bf16[16,16,512]{2,1,0:T(8,128)(2,1)} %bitcast.24), calls=%async_computation | async-start | bytes 524288 | tf_op jit(solution)/shard_map/all_to_all | solution.py:138
  172.7 15.8 %all-to-all-done = bf16[16,16,512]{2,1,0:T(8,128)(2,1)S(1)} async-done(((bf16[16,16,512]{2,1,0:T(8,128)(2,1)}), bf16[16,16,512]{2,1,0:T(8,128)(2,1)S(1)}, u32[]{:S(2)}, u32[]{:S(2)}) %all-to-all-start) | async-done | bytes 262176 | tf_op jit(solution)/shard_map/all_to_all | solution.py:138
  191.7 6.3 %collective-permute-start.5 = (bf16[4,16,24,512]{3,2,1,0:T(8,128)(2,1)}, bf16[4,16,24,512]{3,2,1,0:T(8,128)(2,1)S(1)}, u32[]{:S(2)}, u32[]{:S(2)}) collective-permute-start(bf16[4,16,24,512]{3,2,1,0:T(8,128)(2,1)} %bitcast.101), channel_id=1, source_target_pairs={{0,1},{1,0},{2,3},{3,2},{4,5},{5,4},{6,7},{7,6},{8,9},{9,8},{10,11... | collective-permute-start | bytes 4718600 | tf_op jit(solution)/shard_map/ppermute | solution.py:154
  198.0 3.2 %collective-permute-done.5 = bf16[4,16,24,512]{3,2,1,0:T(8,128)(2,1)S(1)} collective-permute-done((bf16[4,16,24,512]{3,2,1,0:T(8,128)(2,1)}, bf16[4,16,24,512]{3,2,1,0:T(8,128)(2,1)S(1)}, u32[]{:S(2)}, u32[]{:S(2)}) %collective-permute-start.5) | collective-permute-done | bytes 1572896 | tf_op jit(solution)/shard_map/ppermute | solution.py:154
  201.2 1.7 pad_maximum_fusion
  204.7 1.8 copy.74
  207.6 35.7 %all_to_all.10 = bf16[16,16,1024]{2,1,0:T(8,128)(2,1)S(1)} all-to-all(bf16[16,16,1024]{2,1,0:T(8,128)(2,1)S(1)} %bitcast.104), channel_id=1, replica_groups=mesh['clip'=4,'xhi'=2,'zhi'=8,'zlo'=2,'xlo'=2,'core'=2] {'xhi','zhi'}, dimensions={0} | all-to-all | bytes 1048576 | tf_op jit(solution)/shard_map/all_to_all | solution.py:162
  (78 shorter events, 23.0 us)
Async XLA Ops:
  6.5 72.1 %all-gather.7.cloned.1.call-start = ((), (), s32[]{:S(2)}) async-start(), calls=%async_computation.2 | async-start | bytes 1671168 | tf_op jit(solution)/shard_map/all_gather | solution.py:77
  8.9 138.2 %all-gather.9.cloned.1.call-start = ((), (), s32[]{:S(2)}) async-start(), calls=%async_computation.3 | async-start | bytes 5898240 | tf_op jit(solution)/shard_map/all_gather | solution.py:122
  21.4 12.1 %collective-permute-start = (bf16[8,1,1024]{2,0,1:T(8,128)(2,1)S(1)}, bf16[8,1,1024]{2,0,1:T(8,128)(2,1)S(1)}, u32[]{:S(2)}, u32[]{:S(2)}) collective-permute-start(bf16[8,1,1024]{2,0,1:T(8,128)(2,1)S(1)} %copy.64), channel_id=1, source_target_pairs={{0,1},{1,2},{2,3},{4,5},{5,6},{6,7},{8,9},{9,10},{10,11},{12,13},{... | collective-permute-start | bytes 49160 | tf_op jit(solution)/shard_map/ppermute | solution.py:23
  27.9 7.4 %collective-permute-start.1 = (bf16[8,1,1024]{2,0,1:T(8,128)(2,1)S(1)}, bf16[8,1,1024]{2,0,1:T(8,128)(2,1)S(1)}, u32[]{:S(2)}, u32[]{:S(2)}) collective-permute-start(bf16[8,1,1024]{2,0,1:T(8,128)(2,1)S(1)} %copy.65), channel_id=1, source_target_pairs={{1,0},{2,1},{3,2},{5,4},{6,5},{7,6},{9,8},{10,9},{11,10},{13,12},{... | collective-permute-start | bytes 49160 | tf_op jit(solution)/shard_map/ppermute | solution.py:25
  41.4 1.3 copy-start
  42.7 12.1 %collective-permute-start.2 = (bf16[1,34,1024]{1,2,0:T(8,128)(2,1)S(1)}, bf16[1,34,1024]{1,2,0:T(8,128)(2,1)S(1)}, u32[]{:S(2)}, u32[]{:S(2)}) collective-permute-start(bf16[1,34,1024]{1,2,0:T(8,128)(2,1)S(1)} %slice_select_fusion), channel_id=1, source_target_pairs={{0,4},{4,0},{8,12},{12,8},{16,20},{20,16},{24,28},{28,24},{32,36},... | collective-permute-start | bytes 208904 | tf_op jit(solution)/shard_map/ppermute | solution.py:35
  55.3 4.2 %collective-permute-start.3 = (bf16[10,34,1024]{2,1,0:T(8,128)(2,1)S(1)}, bf16[10,34,1024]{2,1,0:T(8,128)(2,1)S(1)}, u32[]{:S(2)}, u32[]{:S(2)}) collective-permute-start(bf16[10,34,1024]{2,1,0:T(8,128)(2,1)S(1)} %pad_maximum_fusion.2), channel_id=1, source_target_pairs={{0,1},{1,0},{2,3},{3,2},{4,5},{5,4},{6,7},{7,6},{8,9},{9,8},{10,11... | collective-permute-start | bytes 2088968 | tf_op jit(solution)/shard_map/ppermute | solution.py:100
  81.0 110.7 %all-gather.11.cloned.1.call-start = ((), (), s32[]{:S(2)}) async-start(), calls=%async_computation.4 | async-start | bytes 1966080 | tf_op jit(solution)/shard_map/all_gather | solution.py:133
  147.1 3.2 %copy-start.2 = (bf16[64,72,512]{2,1,0:T(8,128)(2,1)S(1)}, bf16[64,72,512]{2,1,0:T(8,128)(2,1)}, u32[]{:S(2)}) copy-start(bf16[64,72,512]{2,1,0:T(8,128)(2,1)} %all-gather.9.cloned.1.call-done) | copy-start | bytes 14155780
  148.7 2.0 copy-start.5
  150.3 1.0 copy-start.3
  151.3 1.0 copy-start.7
  151.7 1.1 copy-start.6
  152.3 1.1 copy-start.4
  153.4 19.1 %copy-start.9 = (s32[8]{0:T(128)S(1)}, s32[8]{0:T(128)}, u32[]{:S(2)}) copy-start(s32[8]{0:T(128)} %param.9) | copy-start | bytes 100
  153.4 19.2 %copy-start.8 = (s32[16]{0:T(128)S(1)}, s32[16]{0:T(128)}, u32[]{:S(2)}) copy-start(s32[16]{0:T(128)} %param.8) | copy-start | bytes 196
  153.9 4.1 %collective-permute-start.4 = (f32[256,512]{1,0:T(8,128)S(1)}, f32[256,512]{1,0:T(8,128)S(1)}, u32[]{:S(2)}, u32[]{:S(2)}) collective-permute-start(f32[256,512]{1,0:T(8,128)S(1)} %slice.163), channel_id=1, source_target_pairs={{0,1},{1,0},{2,3},{3,2},{4,5},{5,4},{6,7},{7,6},{8,9},{9,8},{10,11... | collective-permute-start | bytes 1572872 | tf_op jit(solution)/shard_map/ppermute | solution.py:134
  158.9 29.6 %all-to-all-start = ((bf16[16,16,512]{2,1,0:T(8,128)(2,1)}), bf16[16,16,512]{2,1,0:T(8,128)(2,1)S(1)}, u32[]{:S(2)}, u32[]{:S(2)}) async-start(bf16[16,16,512]{2,1,0:T(8,128)(2,1)} %bitcast.24), calls=%async_computation | async-start | bytes 524288 | tf_op jit(solution)/shard_map/all_to_all | solution.py:138
  191.7 9.5 %collective-permute-start.5 = (bf16[4,16,24,512]{3,2,1,0:T(8,128)(2,1)}, bf16[4,16,24,512]{3,2,1,0:T(8,128)(2,1)S(1)}, u32[]{:S(2)}, u32[]{:S(2)}) collective-permute-start(bf16[4,16,24,512]{3,2,1,0:T(8,128)(2,1)} %bitcast.101), channel_id=1, source_target_pairs={{0,1},{1,0},{2,3},{3,2},{4,5},{5,4},{6,7},{7,6},{8,9},{9,8},{10,11... | collective-permute-start | bytes 4718600 | tf_op jit(solution)/shard_map/ppermute | solution.py:154
  206.6 36.8 %copy-start.1 = (bf16[8,32,1024]{2,1,0:T(8,128)(2,1)S(1)}, bf16[8,32,1024]{2,1,0:T(8,128)(2,1)}, u32[]{:S(2)}) copy-start(bf16[8,32,1024]{2,1,0:T(8,128)(2,1)} %param.5) | copy-start | bytes 1572868
Sparse Core Ops, SparseCore 0:
  9.4 69.1 all-gather.6
  81.1 65.9 all-gather.8
  154.0 37.3 all-gather.10

commit v2 on v1

--- a/solution.py
+++ b/solution.py
@@ -119,14 +119,19 @@
     early = 3
     along_z, *head = lax.optimization_barrier((along_z, *patches[:early]))
     patches[:early] = head
-    own_half = lax.all_gather(along_z[:, :spatial_rows], ("xhi", "xlo"), axis=0)
-    own_half = own_half.reshape((-1, spatial_rows) + along_z.shape[2:])
+    cut = 5 * block_in
+    parts = [
+        lax.all_gather(along_z[:, rows], ("xhi", "xlo"), axis=0)
+        for rows in (slice(None, cut), slice(cut, spatial_rows))
+    ]
+    parts = [part.reshape((-1,) + part.shape[2:]) for part in parts]
     temporal_rows = along_z[:, spatial_rows:]
     partial = jnp.zeros((2 * tokens, middle), jnp.float32)
     for tap, patch in enumerate(patches):
+        row = tap * block_in
         partial = partial + jnp.dot(
             patch,
-            own_half[:, tap * block_in : (tap + 1) * block_in, :].reshape(width, middle),
+            parts[row // cut][:, row % cut : row % cut + block_in, :].reshape(width, middle),
             preferred_element_type=jnp.float32,
         )
     partial, temporal_rows = lax.optimization_barrier((partial, temporal_rows))

time: 255 us -> 274 us (1.075)
  waiting for transfers between devices: 108 us -> 122 us
    all_gather x1 -> x2, waiting for transfers between devices: 59.4 us -> 74.8 us  [shards(): lax.all_gather(along_z[:, rows], ('xhi', 'xlo'), axis=0)]
    ppermute x1, starting transfers between devices: 5.57 us -> 8.79 us  [padded_2(): lax.ppermute(head, axis, [((i + 1) % count, i) for i in range(ends)])]
  transfers between devices with their start and end apart: 10 -> 11, of which waited for: 7 -> 8; matrix products, arithmetic and copies ran while one was open for 15% -> 16% of each run, Pallas kernels for 0% -> 0%
where the time goes in v2:
time: 274 us; the launch traced here: 270 us
  waiting for transfers between devices  122 us (45%)
  starting transfers between devices  38.2 us (14%)
  blocking collectives  35.8 us (13%)
  local copies, waits for them, and re-layouts  32 us (12%)
  other arithmetic  19.5 us (7%)
  between operations  13.6 us (5%)
  matrix products  9.2 us (3%)
    all_gather x2, waiting for transfers between devices, shards(): lax.all_gather(along_z[:, rows], ('xhi', 'xlo'), axis=0)  74.8 us
    all_to_all x1, blocking collectives, shards(): lax.all_to_all(mixed_out.reshape(group_size, per_pixel, channels), FRAME_...  35.8 us
    all_gather x1, waiting for transfers between devices, shards(): lax.all_gather(weight_rows(w_spatial, w_temporal), ('zhi', 'zlo'), axis=0)  17 us
    all_to_all x1, waiting for transfers between devices, shards(): lax.all_to_all(hidden.reshape(group_size, per_pixel, middle), FRAME_AXES,...  15.8 us
    all_to_all x1, starting transfers between devices, shards(): lax.all_to_all(hidden.reshape(group_size, per_pixel, middle), FRAME_AXES,...  13.2 us
    ppermute x1, starting transfers between devices, padded_2(): lax.ppermute(head, axis, [((i + 1) % count, i) for i in range(ends)])  8.79 us
    ppermute x1, waiting for transfers between devices, partner(): return lax.ppermute(value, axis, pairs)  7.38 us
    dot_general x9, matrix products, shards(): jnp.dot(patch, parts[row // cut][:, row % cut:row % cut + block_in, :].re...  7.33 us
  transfers between devices with their start and end apart: 11, of which 8 were waited for; matrix products, arithmetic and copies ran while one was open for 16% of the time, Pallas kernels for 0%

profile of v2, /device:TPU:1, one launch (start us, length us, event | category | flops | bytes accessed | tf_op | source)
XLA Modules:
  0.0 270.0 jit_solution(14533330676671642971)
XLA Ops:
  7.3 1.5 pad_maximum_fusion.12
  12.8 1.8 copy.62
  14.5 2.2 copy.63
  16.7 2.7 %fusion.22 = (bf16[8,1,1024]{1,2,0:T(8,128)(2,1)}, bf16[8,1,1024]{1,2,0:T(8,128)(2,1)}) fusion(bf16[8,32,1024]{1,2,0:T(8,128)(2,1)S(1)} %bitcast.83), kind=kLoop, calls=%fused_computation.79 | loop fusion | bytes 65536 | tf_op jit(solution)/shard_map/slice | solution.py:20
  19.4 2.0 copy.65
  21.4 8.8 %collective-permute-start.1 = (bf16[8,1,1024]{2,0,1:T(8,128)(2,1)S(1)}, bf16[8,1,1024]{2,0,1:T(8,128)(2,1)S(1)}, u32[]{:S(2)}, u32[]{:S(2)}) collective-permute-start(bf16[8,1,1024]{2,0,1:T(8,128)(2,1)S(1)} %copy.65), channel_id=1, source_target_pairs={{1,0},{2,1},{3,2},{5,4},{6,5},{7,6},{9,8},{10,9},{11,10},{13,12},{... | collective-permute-start | bytes 49160 | tf_op jit(solution)/shard_map/ppermute | solution.py:25
  30.2 2.0 copy.64
  32.1 1.9 collective-permute-start
  34.1 1.8 copy.67
  35.9 1.8 copy.66
  37.8 4.1 %pad_maximum_fusion.1 = bf16[8,34,1024]{1,2,0:T(8,128)(2,1)S(1)} fusion(bf16[8,1,1024]{1,2,0:T(8,128)(2,1)} %copy.67, bf16[8,32,1024]{1,2,0:T(8,128)(2,1)S(1)} %bitcast.84, bf16[8,1,1024]{1,2,0:T(8,128)(2,1)} %copy.66), kind=kLoop, calls=%fused_computation.2 | loop fusion | flops 1671168 | bytes 1114112 | tf_op jit(solution)/shard_map/concatenate | solution.py:21
  43.3 1.9 collective-permute-start.2
  45.2 2.0 copy.69
  47.2 7.4 %collective-permute-done.2 = bf16[1,34,1024]{1,2,0:T(8,128)(2,1)S(1)} collective-permute-done((bf16[1,34,1024]{1,2,0:T(8,128)(2,1)S(1)}, bf16[1,34,1024]{1,2,0:T(8,128)(2,1)S(1)}, u32[]{:S(2)}, u32[]{:S(2)}) %collective-permute-start.2) | collective-permute-done | bytes 69664 | tf_op jit(solution)/shard_map/ppermute | solution.py:35
  55.1 3.4 %collective-permute-start.3 = (bf16[10,34,1024]{2,1,0:T(8,128)(2,1)S(1)}, bf16[10,34,1024]{2,1,0:T(8,128)(2,1)S(1)}, u32[]{:S(2)}, u32[]{:S(2)}) collective-permute-start(bf16[10,34,1024]{2,1,0:T(8,128)(2,1)S(1)} %pad_maximum_fusion.2), channel_id=1, source_target_pairs={{0,1},{1,0},{2,3},{3,2},{4,5},{5,4},{6,7},{7,6},{8,9},{9,8},{10,11... | collective-permute-start | bytes 2088968 | tf_op jit(solution)/shard_map/ppermute | solution.py:100
  58.6 1.9 collective-permute-done.3
  61.7 17.0 %all-gather.9.cloned.1.call-done = bf16[1536,512]{1,0:T(8,128)(2,1)} async-done(((bf16[96,512]{1,0:T(8,128)(2,1)}), bf16[1536,512]{1,0:T(8,128)(2,1)}) %all-gather.9.cloned.1.call-update) | async-done | bytes 1572880 | tf_op jit(solution)/shard_map/all_gather | solution.py:77
  78.7 2.0 slice.138
  80.8 1.9 slice.152
  87.7 1.8 slice.165
  89.4 39.3 %all-gather.11.cloned.1.call-done = bf16[64,40,512]{2,1,0:T(8,128)(2,1)} async-done(((bf16[16,40,512]{2,1,0:T(8,128)(2,1)}), bf16[64,40,512]{2,1,0:T(8,128)(2,1)}) %all-gather.11.cloned.1.call-update) | async-done | bytes 2621456 | tf_op jit(solution)/shard_map/all_gather | solution.py:124
  130.2 1.6 convolution_add_fusion.7
  134.1 35.5 %all-gather.13.cloned.1.call-done = bf16[64,32,512]{2,1,0:T(8,128)(2,1)} async-done(((bf16[16,32,512]{2,1,0:T(8,128)(2,1)}), bf16[64,32,512]{2,1,0:T(8,128)(2,1)}) %all-gather.13.cloned.1.call-update) | async-done | bytes 2097168 | tf_op jit(solution)/shard_map/all_gather | solution.py:124
  169.6 1.6 convolution_add_fusion.3
  173.4 2.6 collective-permute-start.4
  178.4 13.2 %all-to-all-start = ((bf16[16,16,512]{2,1,0:T(8,128)(2,1)}), bf16[16,16,512]{2,1,0:T(8,128)(2,1)S(1)}, u32[]{:S(2)}, u32[]{:S(2)}) async-start(bf16[16,16,512]{2,1,0:T(8,128)(2,1)} %bitcast.24), calls=%async_computation | async-start | bytes 524288 | tf_op jit(solution)/shard_map/all_to_all | solution.py:143
  191.8 15.8 %all-to-all-done = bf16[16,16,512]{2,1,0:T(8,128)(2,1)S(1)} async-done(((bf16[16,16,512]{2,1,0:T(8,128)(2,1)}), bf16[16,16,512]{2,1,0:T(8,128)(2,1)S(1)}, u32[]{:S(2)}, u32[]{:S(2)}) %all-to-all-start) | async-done | bytes 262176 | tf_op jit(solution)/shard_map/all_to_all | solution.py:143
  210.7 6.3 %collective-permute-start.5 = (bf16[4,16,24,512]{3,2,1,0:T(8,128)(2,1)}, bf16[4,16,24,512]{3,2,1,0:T(8,128)(2,1)S(1)}, u32[]{:S(2)}, u32[]{:S(2)}) collective-permute-start(bf16[4,16,24,512]{3,2,1,0:T(8,128)(2,1)} %bitcast.102), channel_id=1, source_target_pairs={{0,1},{1,0},{2,3},{3,2},{4,5},{5,4},{6,7},{7,6},{8,9},{9,8},{10,11... | collective-permute-start | bytes 4718600 | tf_op jit(solution)/shard_map/ppermute | solution.py:159
  217.0 3.2 %collective-permute-done.5 = bf16[4,16,24,512]{3,2,1,0:T(8,128)(2,1)S(1)} collective-permute-done((bf16[4,16,24,512]{3,2,1,0:T(8,128)(2,1)}, bf16[4,16,24,512]{3,2,1,0:T(8,128)(2,1)S(1)}, u32[]{:S(2)}, u32[]{:S(2)}) %collective-permute-start.5) | collective-permute-done | bytes 1572896 | tf_op jit(solution)/shard_map/ppermute | solution.py:159
  220.2 1.7 pad_maximum_fusion
  223.8 1.8 copy.74
  226.6 35.8 %all_to_all.10 = bf16[16,16,1024]{2,1,0:T(8,128)(2,1)S(1)} all-to-all(bf16[16,16,1024]{2,1,0:T(8,128)(2,1)S(1)} %bitcast.105), channel_id=1, replica_groups=mesh['clip'=4,'xhi'=2,'zhi'=8,'zlo'=2,'xlo'=2,'core'=2] {'xhi','zhi'}, dimensions={0} | all-to-all | bytes 1048576 | tf_op jit(solution)/shard_map/all_to_all | solution.py:167
  (84 shorter events, 28.1 us)
Async XLA Ops:
  6.5 72.2 %all-gather.9.cloned.1.call-start = ((), (), s32[]{:S(2)}) async-start(), calls=%async_computation.2 | async-start | bytes 1671168 | tf_op jit(solution)/shard_map/all_gather | solution.py:77
  8.9 119.8 %all-gather.11.cloned.1.call-start = ((), (), s32[]{:S(2)}) async-start(), calls=%async_computation.3 | async-start | bytes 3276800 | tf_op jit(solution)/shard_map/all_gather | solution.py:124
  21.4 12.7 %collective-permute-start.1 = (bf16[8,1,1024]{2,0,1:T(8,128)(2,1)S(1)}, bf16[8,1,1024]{2,0,1:T(8,128)(2,1)S(1)}, u32[]{:S(2)}, u32[]{:S(2)}) collective-permute-start(bf16[8,1,1024]{2,0,1:T(8,128)(2,1)S(1)} %copy.65), channel_id=1, source_target_pairs={{1,0},{2,1},{3,2},{5,4},{6,5},{7,6},{9,8},{10,9},{11,10},{13,12},{... | collective-permute-start | bytes 49160 | tf_op jit(solution)/shard_map/ppermute | solution.py:25
  32.1 3.8 %collective-permute-start = (bf16[8,1,1024]{2,0,1:T(8,128)(2,1)S(1)}, bf16[8,1,1024]{2,0,1:T(8,128)(2,1)S(1)}, u32[]{:S(2)}, u32[]{:S(2)}) collective-permute-start(bf16[8,1,1024]{2,0,1:T(8,128)(2,1)S(1)} %copy.64), channel_id=1, source_target_pairs={{0,1},{1,2},{2,3},{4,5},{5,6},{6,7},{8,9},{9,10},{10,11},{12,13},{... | collective-permute-start | bytes 49160 | tf_op jit(solution)/shard_map/ppermute | solution.py:23
  41.9 1.3 copy-start
  43.3 11.3 %collective-permute-start.2 = (bf16[1,34,1024]{1,2,0:T(8,128)(2,1)S(1)}, bf16[1,34,1024]{1,2,0:T(8,128)(2,1)S(1)}, u32[]{:S(2)}, u32[]{:S(2)}) collective-permute-start(bf16[1,34,1024]{1,2,0:T(8,128)(2,1)S(1)} %slice_select_fusion), channel_id=1, source_target_pairs={{0,4},{4,0},{8,12},{12,8},{16,20},{20,16},{24,28},{28,24},{32,36},... | collective-permute-start | bytes 208904 | tf_op jit(solution)/shard_map/ppermute | solution.py:35
  55.1 5.3 %collective-permute-start.3 = (bf16[10,34,1024]{2,1,0:T(8,128)(2,1)S(1)}, bf16[10,34,1024]{2,1,0:T(8,128)(2,1)S(1)}, u32[]{:S(2)}, u32[]{:S(2)}) collective-permute-start(bf16[10,34,1024]{2,1,0:T(8,128)(2,1)S(1)} %pad_maximum_fusion.2), channel_id=1, source_target_pairs={{0,1},{1,0},{2,3},{3,2},{4,5},{5,4},{6,7},{7,6},{8,9},{9,8},{10,11... | collective-permute-start | bytes 2088968 | tf_op jit(solution)/shard_map/ppermute | solution.py:100
  80.7 88.8 %all-gather.13.cloned.1.call-start = ((), (), s32[]{:S(2)}) async-start(), calls=%async_computation.4 | async-start | bytes 2621440 | tf_op jit(solution)/shard_map/all_gather | solution.py:124
  82.7 128.0 %all-gather.15.cloned.1.call-start = ((), (), s32[]{:S(2)}) async-start(), calls=%async_computation.5 | async-start | bytes 1966080 | tf_op jit(solution)/shard_map/all_gather | solution.py:138
  130.2 1.9 copy-start.2
  132.1 1.0 copy-start.4
  132.6 1.1 copy-start.3
  134.1 37.1 %copy-start.5 = (bf16[16,32,512]{2,1,0:T(8,128)(2,1)S(1)}, bf16[16,32,512]{2,1,0:T(8,128)(2,1)}, u32[]{:S(2)}) copy-start(bf16[16,32,512]{2,1,0:T(8,128)(2,1)} %pad_maximum_fusion.9) | copy-start | bytes 1572868
  169.6 1.8 copy-start.8
  171.2 1.1 copy-start.6
  171.8 1.1 copy-start.7
  173.3 18.3 %copy-start.10 = (s32[8]{0:T(128)S(1)}, s32[8]{0:T(128)}, u32[]{:S(2)}) copy-start(s32[8]{0:T(128)} %param.9) | copy-start | bytes 100
  173.3 18.4 %copy-start.9 = (s32[16]{0:T(128)S(1)}, s32[16]{0:T(128)}, u32[]{:S(2)}) copy-start(s32[16]{0:T(128)} %param.8) | copy-start | bytes 196
  173.4 4.1 %collective-permute-start.4 = (f32[256,512]{1,0:T(8,128)S(1)}, f32[256,512]{1,0:T(8,128)S(1)}, u32[]{:S(2)}, u32[]{:S(2)}) collective-permute-start(f32[256,512]{1,0:T(8,128)S(1)} %slice.167), channel_id=1, source_target_pairs={{0,1},{1,0},{2,3},{3,2},{4,5},{5,4},{6,7},{7,6},{8,9},{9,8},{10,11... | collective-permute-start | bytes 1572872 | tf_op jit(solution)/shard_map/ppermute | solution.py:139
  178.4 29.2 %all-to-all-start = ((bf16[16,16,512]{2,1,0:T(8,128)(2,1)}), bf16[16,16,512]{2,1,0:T(8,128)(2,1)S(1)}, u32[]{:S(2)}, u32[]{:S(2)}) async-start(bf16[16,16,512]{2,1,0:T(8,128)(2,1)} %bitcast.24), calls=%async_computation | async-start | bytes 524288 | tf_op jit(solution)/shard_map/all_to_all | solution.py:143
  210.7 9.5 %collective-permute-start.5 = (bf16[4,16,24,512]{3,2,1,0:T(8,128)(2,1)}, bf16[4,16,24,512]{3,2,1,0:T(8,128)(2,1)S(1)}, u32[]{:S(2)}, u32[]{:S(2)}) collective-permute-start(bf16[4,16,24,512]{3,2,1,0:T(8,128)(2,1)} %bitcast.102), channel_id=1, source_target_pairs={{0,1},{1,0},{2,3},{3,2},{4,5},{5,4},{6,7},{7,6},{8,9},{9,8},{10,11... | collective-permute-start | bytes 4718600 | tf_op jit(solution)/shard_map/ppermute | solution.py:159
  225.6 36.8 %copy-start.1 = (bf16[8,32,1024]{2,1,0:T(8,128)(2,1)S(1)}, bf16[8,32,1024]{2,1,0:T(8,128)(2,1)}, u32[]{:S(2)}) copy-start(bf16[8,32,1024]{2,1,0:T(8,128)(2,1)} %param.5) | copy-start | bytes 1572868
Sparse Core Ops, SparseCore 0:
  9.4 69.2 all-gather.8
  80.9 47.8 all-gather.10
  130.8 38.6 all-gather.12
  173.4 36.9 all-gather.14
